TPU v7x, 32 devices: a whole 2x2x4 slice. The times are simulated.
32 devices in a mesh: sector: 8 (over y, x, core), sub: 4 (over z).
Axes of the slice: x: 2, y: 2, z: 4, core: 2. Of those that a mesh axis runs over, the one named last changes fastest.
Arguments:
- dual_load: float32 [8, 4, 2, 512, 256], P('sector', 'sub'), may hold values from -50 to 50
- flexibility: bfloat16 [8, 4, 2048, 2048], P('sector', 'sub'), may hold values from -10 to 10, as said below
- face_order: int32 [8, 4, 2048], P('sector', 'sub'), may hold values from 0 to 2047, each once within a row
- corner_index: int32 [8, 4, 32], P('sector', 'sub'), may hold values from 0 to 2047, as said below
- coarse_inverse: float32 [256, 256], replicated, may hold values from -10 to 10, as said below
Outputs:
- multiplier: float32 [8, 4, 2, 512, 256], P('sector', 'sub')
- residual: float32 [8, 4, 2, 512, 256], P('sector', 'sub')
Inputs may be any that keep to these rules, and one draw needn't show every extreme that they name: `flexibility`: a block of sizes of order one with a dominant diagonal; each subdomain's matrix is symmetric positive definite. `corner_index`: entries within one subdomain are distinct. `face_order`: each subdomain's row names every face slot once. `coarse_inverse`: symmetric positive definite with a dominant diagonal.
All inputs are finite; a program needn't handle non-finite values.
Results may differ from a plain program's by a relative error of at most 0.0087.
The roundings to bfloat16 on the way count: a program that leaves them out, or rounds other values in their place, can miss the bound.
Values may be sent and summed in bfloat16 or wider, within the bound.
No kernel may reach another device: no remote copies, remote signals or barrier semaphores. Data moves between devices by JAX's collectives and lax.ppermute only.
A program may use at most 128 MiB of HBM per device.

v0:
```python
import jax
import jax.numpy as jnp
from jax import lax
from jax.sharding import PartitionSpec as P

ITERS = 2


def passed_along(x, axis, by):
    count = lax.axis_size(axis)
    pairs = [(i, i + by) for i in range(count) if 0 <= i + by < count]
    return lax.ppermute(x, axis, pairs)


def from_behind(value, axis, steps):
    count = lax.axis_size(axis)
    pairs = [(source, (source + steps) % count) for source in range(count)]
    return lax.ppermute(value, axis, pairs)


def squares(residual):
    return lax.psum(jnp.sum(residual * residual, axis=(0, 1, 2, 3)), ("sector", "sub"))


def inner_sum(left, right):
    return jnp.sum(left * right, axis=(0, 1, 2, 3))


def shards(dual_load, flexibility, face_order, corner_index, coarse_inverse):
    slot_order = face_order[0, 0]
    corners = corner_index[0, 0]
    corner_count = corners.shape[0]
    matrix = jnp.take(jnp.take(flexibility[0, 0], slot_order, axis=0), slot_order, axis=1)
    face_width = slot_order.shape[0] // 4
    cases = dual_load.shape[-1]
    sub_count = lax.axis_size("sub")
    multiplier = jnp.zeros_like(dual_load)
    residual = dual_load
    direction = dual_load
    norm_now = squares(residual)
    for iteration in range(ITERS):
        rounded = direction[0, 0].astype(jnp.bfloat16)
        lower_sub = passed_along(rounded[0], "sub", 1)
        previous = from_behind(rounded[1], "sector", 1)
        face_stack = jnp.concatenate([-lower_sub, rounded[0], -previous, rounded[1]], axis=0)
        partial_value = jnp.take(face_stack, corners, axis=0).astype(jnp.float32)
        sector_total = lax.psum(partial_value.astype(jnp.bfloat16), "sub").astype(jnp.float32)
        sector_id = lax.axis_index("sector")
        everything = lax.all_gather(sector_total, "sector", axis=0, tiled=True)
        inverse_rows = lax.dynamic_slice_in_dim(
            coarse_inverse, sector_id * corner_count, corner_count, 0
        )
        coarse = jnp.dot(
            inverse_rows,
            everything,
            precision=lax.Precision.HIGHEST,
            preferred_element_type=jnp.float32,
        )
        coarse = coarse / sub_count
        correction = jnp.zeros((4 * face_width, cases), jnp.float32).at[corners].add(coarse)
        product = jnp.dot(matrix, face_stack, preferred_element_type=jnp.float32) + correction
        outgoing_sub = product[:face_width]
        outgoing_cycle = product[2 * face_width : 3 * face_width]
        upper_next = passed_along(outgoing_sub.astype(jnp.bfloat16), "sub", -1)
        cycle_next = from_behind(outgoing_cycle.astype(jnp.bfloat16), "sector", -1)
        own_sub = product[face_width : 2 * face_width]
        own_cycle = product[3 * face_width :]
        jump_pair = jnp.stack(
            [own_sub - upper_next.astype(jnp.float32), own_cycle - cycle_next.astype(jnp.float32)],
            axis=0,
        )
        image = jump_pair[None, None]
        curvature = lax.psum(inner_sum(direction, image), ("sector", "sub"))
        alpha = norm_now / curvature
        multiplier = multiplier + alpha * direction
        residual = residual - alpha * image
        if iteration + 1 < ITERS:
            norm_next = squares(residual)
            direction = residual + norm_next / norm_now * direction
            norm_now = norm_next
    return (multiplier, residual)


def solution(mesh):
    return jax.shard_map(
        shards,
        mesh=mesh,
        in_specs=(
            P("sector", "sub", None, None, None),
            P("sector", "sub", None, None),
            P("sector", "sub", None),
            P("sector", "sub", None),
            P(),
        ),
        out_specs=(P("sector", "sub", None, None, None), P("sector", "sub", None, None, None)),
        check_vma=False,
    )
```

profile of v0, /device:TPU:10, one launch (start us, length us, event | category | flops | bytes accessed | tf_op | source)
XLA Modules:
  0.0 299.7 jit_solution(9664023918029677284)
XLA Ops:
  0.7 1.3 convert_element_type.34
  2.1 3.5 %collective-permute-start = (bf16[512,256]{1,0:T(8,128)(2,1)S(1)}, bf16[512,256]{1,0:T(8,128)(2,1)S(1)}, u32[]{:S(2)}, u32[]{:S(2)}) collective-permute-start(bf16[512,256]{1,0:T(8,128)(2,1)S(1)} %get-tuple-element.27), channel_id=1, source_target_pairs={{0,1},{1,2},{2,3},{4,5},{5,6},{6,7},{8,9},{9,10},{10,11},{12,13},{... | collective-permute-start | bytes 786440 | tf_op jit(solution)/shard_map/ppermute | solution.py:12
  5.7 20.8 %gather_fusion = bf16[2048,2048]{1,0:T(8,128)(2,1)} fusion(bf16[2048,2048]{1,0:T(8,128)(2,1)} %bitcast.51, s32[2048]{0:T(1024)S(1)} %broadcast_clamp_fusion), kind=kCustom, calls=%fused_computation.2 | custom fusion | bytes 16785408 | tf_op jit(solution)/shard_map/jit(_take)/gather | solution.py:33
  26.5 7.4 %broadcast_select_fusion = bf16[2048,2048]{1,0:T(8,128)(2,1)} fusion(bf16[2048,2048]{1,0:T(8,128)(2,1)} %gather_fusion, pred[2048]{0:T(1024)(128)(4,1)S(1)} %compare_and_fusion), kind=kLoop, calls=%fused_computation.6 | loop fusion | flops 4194304 | bytes 16779264 | tf_op jit(solution)/shard_map/jit(_take)/select_n | solution.py:33
  33.9 12.3 %copy.8 = bf16[2048,2048]{0,1:T(8,128)(2,1)} copy(bf16[2048,2048]{1,0:T(8,128)(2,1)} %broadcast_select_fusion) | data formatting | bytes 16777216 | tf_op jit(solution)/shard_map/jit(_take)/select_n | solution.py:33
  46.3 20.8 %gather_fusion.1 = bf16[2048,2048]{1,0:T(8,128)(2,1)} fusion(bf16[2048,2048]{0,1:T(8,128)(2,1)} %copy.8, s32[2048]{0:T(1024)S(1)} %broadcast_clamp_fusion), kind=kCustom, calls=%fused_computation.3 | custom fusion | bytes 16785408 | tf_op jit(solution)/shard_map/jit(_take)/gather | solution.py:33
  67.3 6.5 %fusion = f32[2048,256]{1,0:T(8,128)S(1)} fusion(bf16[2048,2048]{1,0:T(8,128)(2,1)} %gather_fusion.1, pred[2048]{0:T(1024)(128)(4,1)S(1)} %compare_and_fusion, bf16[512,256]{1,0:T(8,128)(2,1)} %copy-done.5, bf16[512,256]{1,0:T(8,128)(2,1)S(1)} %neg.13, bf16[512,256]{1,0:T(8,128)(2,1)} %copy-done.4, bf16[512,256]{1,0:T(8,128)(2,1)S(1)} %neg.12), kind=kOutput, calls=%fused_computation.8 | convolution fusion | flops 2155872256 | bytes 11536384 | tf_op jit(solution)/shard_map/dot_general | solution.py:61
  73.8 0.6 gather_fusion.2
  74.5 14.2 %psum.43 = bf16[32,256]{1,0:T(8,128)(2,1)S(1)} all-reduce(bf16[32,256]{1,0:T(8,128)(2,1)S(1)} %broadcast_select_fusion.5), channel_id=1, replica_groups=mesh['sector'=8,'sub'=4] {'sub'}, use_global_device_ids=true, to_apply=%region_2.4 | all-reduce | flops 8192 | bytes 32768 | tf_op jit(solution)/shard_map/psum | solution.py:47
  88.7 9.3 %all_gather.6 = f32[256,256]{1,0:T(8,128)S(1)} all-gather(f32[32,256]{1,0:T(8,128)S(1)} %convert_element_type.35), channel_id=1, replica_groups=mesh['sector'=8,'sub'=4] {'sector'}, dimensions={0}, use_global_device_ids=true | all-gather | bytes 294912 | tf_op jit(solution)/shard_map/all_gather | solution.py:49
  98.3 1.5 scatter_fusion
  100.0 1.2 copy-done.3
  101.2 5.2 %collective-permute-start.2 = (bf16[512,256]{1,0:T(8,128)(2,1)S(1)}, bf16[512,256]{1,0:T(8,128)(2,1)S(1)}, u32[]{:S(2)}, u32[]{:S(2)}) collective-permute-start(bf16[512,256]{1,0:T(8,128)(2,1)S(1)} %get-tuple-element.23), channel_id=1, source_target_pairs={{1,0},{2,1},{3,2},{5,4},{6,5},{7,6},{9,8},{10,9},{11,10},{13,12},{... | collective-permute-start | bytes 786440 | tf_op jit(solution)/shard_map/ppermute | solution.py:12
  106.4 0.3 collective-permute-start.3
  106.7 5.8 %collective-permute-done.2 = bf16[512,256]{1,0:T(8,128)(2,1)S(1)} collective-permute-done((bf16[512,256]{1,0:T(8,128)(2,1)S(1)}, bf16[512,256]{1,0:T(8,128)(2,1)S(1)}, u32[]{:S(2)}, u32[]{:S(2)}) %collective-permute-start.2) | collective-permute-done | bytes 262176 | tf_op jit(solution)/shard_map/ppermute | solution.py:12
  112.5 1.4 fusion.9
  114.1 41.2 %all-reduce = (f32[256]{0:T(256)S(1)}, f32[256]{0:T(256)S(1)}) all-reduce(f32[256]{0:T(256)S(1)} %get-tuple-element.4, f32[256]{0:T(256)S(1)} %get-tuple-element.3), channel_id=1, replica_groups=mesh['sector'=8,'sub'=4] {'sector','sub'}, use_global_device_ids=true, to_apply=%region_1.2 | all-reduce | flops 512 | bytes 4096 | tf_op jit(solution)/shard_map/psum | solution.py:22
  155.5 39.3 %psum.45 = f32[256]{0:T(256)S(1)} all-reduce(f32[256]{0:T(256)S(1)} %multiply_reduce_fusion), channel_id=1, replica_groups=mesh['sector'=8,'sub'=4] {'sector','sub'}, use_global_device_ids=true, to_apply=%region_7.9 | all-reduce | flops 256 | bytes 2048 | tf_op jit(solution)/shard_map/psum | solution.py:22
  195.1 2.6 collective-permute-start.4
  197.7 3.2 %collective-permute-done.5 = bf16[512,256]{1,0:T(8,128)(2,1)S(1)} collective-permute-done((bf16[512,256]{1,0:T(8,128)(2,1)S(1)}, bf16[512,256]{1,0:T(8,128)(2,1)S(1)}, u32[]{:S(2)}, u32[]{:S(2)}) %collective-permute-start.5) | collective-permute-done | bytes 262176 | tf_op jit(solution)/shard_map/ppermute | solution.py:18
  201.0 4.7 %collective-permute-done.4 = bf16[512,256]{1,0:T(8,128)(2,1)S(1)} collective-permute-done((bf16[512,256]{1,0:T(8,128)(2,1)S(1)}, bf16[512,256]{1,0:T(8,128)(2,1)S(1)}, u32[]{:S(2)}, u32[]{:S(2)}) %collective-permute-start.4) | collective-permute-done | bytes 262176 | tf_op jit(solution)/shard_map/ppermute | solution.py:12
  205.7 7.8 %fusion.1 = f32[2048,256]{1,0:T(8,128)} fusion(bf16[2048,2048]{1,0:T(8,128)(2,1)} %gather_fusion.1, pred[2048]{0:T(1024)(128)(4,1)S(1)} %compare_and_fusion, bf16[512,256]{1,0:T(8,128)(2,1)S(1)} %get-tuple-element.26, bf16[512,256]{1,0:T(8,128)(2,1)S(1)} %neg.15, bf16[512,256]{1,0:T(8,128)(2,1)S(1)} %get-tuple-element.25, bf16[512,256]{1,0:T(8,128)(2,1)S(1)} %neg.14), kind=kOutput, calls=%fused_computation.9 | convolution fusion | flops 2155872256 | bytes 11536384 | tf_op jit(solution)/shard_map/dot_general | solution.py:61
  213.6 0.6 gather_fusion.3
  214.3 14.9 %psum.46 = bf16[32,256]{1,0:T(8,128)(2,1)S(1)} all-reduce(bf16[32,256]{1,0:T(8,128)(2,1)S(1)} %broadcast_select_fusion.4), channel_id=1, replica_groups=mesh['sector'=8,'sub'=4] {'sub'}, use_global_device_ids=true, to_apply=%region_8.10 | all-reduce | flops 8192 | bytes 32768 | tf_op jit(solution)/shard_map/psum | solution.py:47
  229.2 8.8 %all_gather.7 = f32[256,256]{1,0:T(8,128)S(1)} all-gather(f32[32,256]{1,0:T(8,128)S(1)} %convert_element_type.39), channel_id=1, replica_groups=mesh['sector'=8,'sub'=4] {'sector'}, dimensions={0}, use_global_device_ids=true | all-gather | bytes 294912 | tf_op jit(solution)/shard_map/all_gather | solution.py:49
  238.2 3.7 %scatter_fusion.1 = f32[2048,256]{1,0:T(8,128)} fusion(f32[2048,256]{1,0:T(8,128)} %fusion.1, s32[32]{0:T(128)S(1)} %fusion.19, f32[32,256]{1,0:T(8,128)S(1)} %convolution_multiply_fusion), kind=kCustom, calls=%fused_computation.5 | custom fusion | flops 8192 | bytes 98432 | tf_op jit(solution)/shard_map/scatter-add | solution.py:60
  241.9 1.8 convert.9
  243.8 6.0 %collective-permute-start.6 = (bf16[512,256]{1,0:T(8,128)(2,1)S(1)}, bf16[512,256]{1,0:T(8,128)(2,1)S(1)}, u32[]{:S(2)}, u32[]{:S(2)}) collective-permute-start(bf16[512,256]{1,0:T(8,128)(2,1)S(1)} %get-tuple-element.21), channel_id=1, source_target_pairs={{1,0},{2,1},{3,2},{5,4},{6,5},{7,6},{9,8},{10,9},{11,10},{13,12},{... | collective-permute-start | bytes 786440 | tf_op jit(solution)/shard_map/ppermute | solution.py:12
  249.8 1.1 collective-permute-start.7
  250.9 4.9 %collective-permute-done.6 = bf16[512,256]{1,0:T(8,128)(2,1)S(1)} collective-permute-done((bf16[512,256]{1,0:T(8,128)(2,1)S(1)}, bf16[512,256]{1,0:T(8,128)(2,1)S(1)}, u32[]{:S(2)}, u32[]{:S(2)}) %collective-permute-start.6) | collective-permute-done | bytes 262176 | tf_op jit(solution)/shard_map/ppermute | solution.py:12
  256.3 41.8 %psum.47 = f32[256]{0:T(256)S(1)} all-reduce(f32[256]{0:T(256)S(1)} %fusion.6), channel_id=1, replica_groups=mesh['sector'=8,'sub'=4] {'sector','sub'}, use_global_device_ids=true, to_apply=%region_11.13 | all-reduce | flops 256 | bytes 2048 | tf_op jit(solution)/shard_map/psum | solution.py:73
  298.1 1.6 fusion.7
  (53 shorter events, 2.5 us)
Async XLA Ops:
  0.6 97.4 %copy-start = (f32[256,256]{1,0:T(8,128)S(1)}, f32[256,256]{1,0:T(8,128)}, u32[]{:S(2)}) copy-start(f32[256,256]{1,0:T(8,128)} %param.11) | copy-start | bytes 786436
  0.6 5.0 %copy-start.7 = (s32[1,1,32]{2,1,0:T(1,128)S(1)}, s32[1,1,32]{2,1,0:T(1,128)}, u32[]{:S(2)}) copy-start(s32[1,1,32]{2,1,0:T(1,128)} %param.10) | copy-start | bytes 388
  0.7 5.0 %copy-start.6 = (s32[1,1,2048]{2,1,0:T(1,128)S(1)}, s32[1,1,2048]{2,1,0:T(1,128)}, u32[]{:S(2)}) copy-start(s32[1,1,2048]{2,1,0:T(1,128)} %param.9) | copy-start | bytes 24580
  2.0 65.2 %copy-start.4 = (bf16[512,256]{1,0:T(8,128)(2,1)}, bf16[512,256]{1,0:T(8,128)(2,1)S(1)}, u32[]{:S(2)}) copy-start(bf16[512,256]{1,0:T(8,128)(2,1)S(1)} %get-tuple-element.27) | copy-start | bytes 786436
  2.0 65.2 %copy-start.5 = (bf16[512,256]{1,0:T(8,128)(2,1)}, bf16[512,256]{1,0:T(8,128)(2,1)S(1)}, u32[]{:S(2)}) copy-start(bf16[512,256]{1,0:T(8,128)(2,1)S(1)} %get-tuple-element.28) | copy-start | bytes 786436
  2.1 65.0 %collective-permute-start.1 = (bf16[512,256]{1,0:T(8,128)(2,1)S(1)}, bf16[512,256]{1,0:T(8,128)(2,1)S(1)}, u32[]{:S(2)}, u32[]{:S(2)}) collective-permute-start(bf16[512,256]{1,0:T(8,128)(2,1)S(1)} %get-tuple-element.28), channel_id=1, source_target_pairs={{0,4},{4,8},{8,12},{12,16},{16,20},{20,24},{24,28},{28,0},{1,5},{5... | collective-permute-start | bytes 786440 | tf_op jit(solution)/shard_map/ppermute | solution.py:18
  2.1 65.0 %collective-permute-start = (bf16[512,256]{1,0:T(8,128)(2,1)S(1)}, bf16[512,256]{1,0:T(8,128)(2,1)S(1)}, u32[]{:S(2)}, u32[]{:S(2)}) collective-permute-start(bf16[512,256]{1,0:T(8,128)(2,1)S(1)} %get-tuple-element.27), channel_id=1, source_target_pairs={{0,1},{1,2},{2,3},{4,5},{5,6},{6,7},{8,9},{9,10},{10,11},{12,13},{... | collective-permute-start | bytes 786440 | tf_op jit(solution)/shard_map/ppermute | solution.py:12
  99.8 1.4 copy-start.3
  101.2 12.6 %copy-start.1 = (f32[1,1,2,512,256]{4,3,2,1,0:T(8,128)S(1)}, f32[1,1,2,512,256]{4,3,2,1,0:T(8,128)}, u32[]{:S(2)}) copy-start(f32[1,1,2,512,256]{4,3,2,1,0:T(8,128)} %param.7) | copy-start | bytes 3145732
  101.2 11.3 %collective-permute-start.2 = (bf16[512,256]{1,0:T(8,128)(2,1)S(1)}, bf16[512,256]{1,0:T(8,128)(2,1)S(1)}, u32[]{:S(2)}, u32[]{:S(2)}) collective-permute-start(bf16[512,256]{1,0:T(8,128)(2,1)S(1)} %get-tuple-element.23), channel_id=1, source_target_pairs={{1,0},{2,1},{3,2},{5,4},{6,5},{7,6},{9,8},{10,9},{11,10},{13,12},{... | collective-permute-start | bytes 786440 | tf_op jit(solution)/shard_map/ppermute | solution.py:12
  106.4 6.1 %collective-permute-start.3 = (bf16[512,256]{1,0:T(8,128)(2,1)S(1)}, bf16[512,256]{1,0:T(8,128)(2,1)S(1)}, u32[]{:S(2)}, u32[]{:S(2)}) collective-permute-start(bf16[512,256]{1,0:T(8,128)(2,1)S(1)} %get-tuple-element.24), channel_id=1, source_target_pairs={{0,28},{4,0},{8,4},{12,8},{16,12},{20,16},{24,20},{28,24},{1,29},{... | collective-permute-start | bytes 786440 | tf_op jit(solution)/shard_map/ppermute | solution.py:18
  195.1 5.8 %collective-permute-start.5 = (bf16[512,256]{1,0:T(8,128)(2,1)S(1)}, bf16[512,256]{1,0:T(8,128)(2,1)S(1)}, u32[]{:S(2)}, u32[]{:S(2)}) collective-permute-start(bf16[512,256]{1,0:T(8,128)(2,1)S(1)} %get-tuple-element.26), channel_id=1, source_target_pairs={{0,4},{4,8},{8,12},{12,16},{16,20},{20,24},{24,28},{28,0},{1,5},{5... | collective-permute-start | bytes 786440 | tf_op jit(solution)/shard_map/ppermute | solution.py:18
  195.1 10.5 %collective-permute-start.4 = (bf16[512,256]{1,0:T(8,128)(2,1)S(1)}, bf16[512,256]{1,0:T(8,128)(2,1)S(1)}, u32[]{:S(2)}, u32[]{:S(2)}) collective-permute-start(bf16[512,256]{1,0:T(8,128)(2,1)S(1)} %get-tuple-element.25), channel_id=1, source_target_pairs={{0,1},{1,2},{2,3},{4,5},{5,6},{6,7},{8,9},{9,10},{10,11},{12,13},{... | collective-permute-start | bytes 786440 | tf_op jit(solution)/shard_map/ppermute | solution.py:12
  241.9 14.0 %copy-start.2 = (f32[2048,256]{1,0:T(8,128)S(1)}, f32[2048,256]{1,0:T(8,128)}, u32[]{:S(2)}) copy-start(f32[2048,256]{1,0:T(8,128)} %scatter_fusion.1) | copy-start | bytes 6291460
  243.8 12.1 %collective-permute-start.6 = (bf16[512,256]{1,0:T(8,128)(2,1)S(1)}, bf16[512,256]{1,0:T(8,128)(2,1)S(1)}, u32[]{:S(2)}, u32[]{:S(2)}) collective-permute-start(bf16[512,256]{1,0:T(8,128)(2,1)S(1)} %get-tuple-element.21), channel_id=1, source_target_pairs={{1,0},{2,1},{3,2},{5,4},{6,5},{7,6},{9,8},{10,9},{11,10},{13,12},{... | collective-permute-start | bytes 786440 | tf_op jit(solution)/shard_map/ppermute | solution.py:12
  249.8 6.1 %collective-permute-start.7 = (bf16[512,256]{1,0:T(8,128)(2,1)S(1)}, bf16[512,256]{1,0:T(8,128)(2,1)S(1)}, u32[]{:S(2)}, u32[]{:S(2)}) collective-permute-start(bf16[512,256]{1,0:T(8,128)(2,1)S(1)} %get-tuple-element.22), channel_id=1, source_target_pairs={{0,28},{4,0},{8,4},{12,8},{16,12},{20,16},{24,20},{28,24},{1,29},{... | collective-permute-start | bytes 786440 | tf_op jit(solution)/shard_map/ppermute | solution.py:18
where the time goes:
time: 301 us; the launch traced here: 300 us
  blocking collectives  170 us (56%)
  local copies, waits for them, and re-layouts  56.6 us (19%)
  other arithmetic  20.5 us (7%)
  starting transfers between devices  18.8 us (6%)
  waiting for transfers between devices  18.6 us (6%)
  matrix products  14.8 us (5%)
    psum x2, blocking collectives, squares(): lax.psum(jnp.sum(residual * residual, axis=(0, 1, 2, 3)), ('sector', 'sub'))  80.5 us
    psum x1, blocking collectives, shards(): curvature = lax.psum(inner_sum(direction, image), ('sector', 'sub'))  41.8 us
    psum x2, blocking collectives, shards(): lax.psum(partial_value.astype(jnp.bfloat16), 'sub').astype(jnp.float32)  29.2 us
    gather x1, local copies, waits for them, and re-layouts, shards(): jnp.take(flexibility[0, 0], slot_order, axis=0)  20.8 us
    gather x1, local copies, waits for them, and re-layouts, shards(): jnp.take(jnp.take(flexibility[0, 0], slot_order, axis=0), slot_order, axi...  20.8 us
    all_gather x2, blocking collectives, shards(): everything = lax.all_gather(sector_total, 'sector', axis=0, tiled=True)  18.1 us
    ppermute x4, starting transfers between devices, passed_along(): return lax.ppermute(x, axis, pairs)  17.2 us
    ppermute x4, waiting for transfers between devices, passed_along(): return lax.ppermute(x, axis, pairs)  15.4 us
  transfers between devices with their start and end apart: 8, of which 4 were waited for; matrix products, arithmetic and copies ran while one was open for 21% of the time, Pallas kernels for 0%

commit v1 on v0

--- a/solution.py
+++ b/solution.py
@@ -46,7 +46,20 @@
         partial_value = jnp.take(face_stack, corners, axis=0).astype(jnp.float32)
         sector_total = lax.psum(partial_value.astype(jnp.bfloat16), "sub").astype(jnp.float32)
         sector_id = lax.axis_index("sector")
-        everything = lax.all_gather(sector_total, "sector", axis=0, tiled=True)
+        fan = lax.axis_size("sector")
+        pile = [(s, (s + 1) % fan) for s in range(fan)]
+        items = [(s, (s - 1) % fan) for s in range(fan)]
+        oldest, far_arr = ([sector_total], [sector_total])
+        for _ in range(fan // 2):
+            oldest.append(lax.ppermute(oldest[-1], "sector", pile))
+        for _ in tuple(range((fan - 1) // 2)):
+            w1 = lax.ppermute(far_arr[-1], "sector", items)
+            far_arr.append(w1)
+        everything = jnp.roll(
+            jnp.concatenate([*oldest[::-1], *far_arr[1:]], axis=0),
+            (lax.axis_index("sector") - fan // 2) * sector_total.shape[0],
+            axis=0,
+        )
         inverse_rows = lax.dynamic_slice_in_dim(
             coarse_inverse, sector_id * corner_count, corner_count, 0
         )

time: 301 us -> 319 us (1.060)
  waiting for transfers between devices: 18.6 us -> 35.2 us
  blocking collectives: 170 us -> 156 us
  starting transfers between devices: 18.8 us -> 29.7 us
    all_gather x2 -> x0, blocking collectives: 18.1 us -> none  [shards(): everything = lax.all_gather(sector_total, 'sector', axis=0, tiled=True)]
    ppermute x0 -> x14, waiting for transfers between devices: none -> 12.4 us  [the longest x8 6.52 us: shards(): oldest.append(lax.ppermute(oldest[-1], 'sector', pile))]
    ppermute x0 -> x14, starting transfers between devices: none -> 10.6 us  [the longest x6 5.69 us: shards(): w1 = lax.ppermute(far_arr[-1], 'sector', items)]
    psum x2, blocking collectives: 80.5 us -> 84 us  [squares(): lax.psum(jnp.sum(residual * residual, axis=(0, 1, 2, 3)), ('sector', 'sub'))]
  transfers between devices with their start and end apart: 8 -> 22, of which waited for: 4 -> 13; matrix products, arithmetic and copies ran while one was open for 21% -> 24% of each run, Pallas kernels for 0% -> 0%
where the time goes in v1:
time: 319 us; the launch traced here: 316 us
  blocking collectives  156 us (49%)
  local copies, waits for them, and re-layouts  57.4 us (18%)
  waiting for transfers between devices  35.2 us (11%)
  starting transfers between devices  29.7 us (9%)
  other arithmetic  21.2 us (7%)
  matrix products  14.9 us (5%)
    psum x2, blocking collectives, squares(): lax.psum(jnp.sum(residual * residual, axis=(0, 1, 2, 3)), ('sector', 'sub'))  84 us
    psum x1, blocking collectives, shards(): curvature = lax.psum(inner_sum(direction, image), ('sector', 'sub'))  43.5 us
    psum x2, blocking collectives, shards(): lax.psum(partial_value.astype(jnp.bfloat16), 'sub').astype(jnp.float32)  28.9 us
    gather x1, local copies, waits for them, and re-layouts, shards(): jnp.take(flexibility[0, 0], slot_order, axis=0)  20.8 us
    gather x1, local copies, waits for them, and re-layouts, shards(): jnp.take(jnp.take(flexibility[0, 0], slot_order, axis=0), slot_order, axi...  20.8 us
    ppermute x4, starting transfers between devices, passed_along(): return lax.ppermute(x, axis, pairs)  18.1 us
    ppermute x4, waiting for transfers between devices, passed_along(): return lax.ppermute(x, axis, pairs)  16.7 us
    dot_general x2, matrix products, shards(): jnp.dot(matrix, face_stack, preferred_element_type=jnp.float32) + correction  14.4 us
  transfers between devices with their start and end apart: 22, of which 13 were waited for; matrix products, arithmetic and copies ran while one was open for 24% of the time, Pallas kernels for 0%

profile of v1, /device:TPU:10, one launch (start us, length us, event | category | flops | bytes accessed | tf_op | source)
XLA Modules:
  0.0 316.1 jit_solution(9323652276445208473)
XLA Ops:
  2.1 3.5 %collective-permute-start = (bf16[512,256]{1,0:T(8,128)(2,1)S(1)}, bf16[512,256]{1,0:T(8,128)(2,1)S(1)}, u32[]{:S(2)}, u32[]{:S(2)}) collective-permute-start(bf16[512,256]{1,0:T(8,128)(2,1)S(1)} %get-tuple-element.28), channel_id=1, source_target_pairs={{0,1},{1,2},{2,3},{4,5},{5,6},{6,7},{8,9},{9,10},{10,11},{12,13},{... | collective-permute-start | bytes 786440 | tf_op jit(solution)/shard_map/ppermute | solution.py:12
  5.7 2.2 collective-permute-done.1
  7.9 4.6 %collective-permute-done = bf16[512,256]{1,0:T(8,128)(2,1)S(1)} collective-permute-done((bf16[512,256]{1,0:T(8,128)(2,1)S(1)}, bf16[512,256]{1,0:T(8,128)(2,1)S(1)}, u32[]{:S(2)}, u32[]{:S(2)}) %collective-permute-start) | collective-permute-done | bytes 262176 | tf_op jit(solution)/shard_map/ppermute | solution.py:12
  13.4 15.4 %psum.43 = bf16[32,256]{1,0:T(8,128)(2,1)S(1)} all-reduce(bf16[32,256]{1,0:T(8,128)(2,1)S(1)} %broadcast_select_fusion.5), channel_id=1, replica_groups=mesh['sector'=8,'sub'=4] {'sub'}, use_global_device_ids=true, to_apply=%region_2.4 | all-reduce | flops 8192 | bytes 32768 | tf_op jit(solution)/shard_map/psum | solution.py:47
  28.9 20.8 %gather_fusion = bf16[2048,2048]{1,0:T(8,128)(2,1)} fusion(bf16[2048,2048]{1,0:T(8,128)(2,1)} %bitcast.49, s32[2048]{0:T(1024)S(1)} %broadcast_clamp_fusion), kind=kCustom, calls=%fused_computation.2 | custom fusion | bytes 16785408 | tf_op jit(solution)/shard_map/jit(_take)/gather | solution.py:33
  49.7 1.6 collective-permute-start.3
  51.3 7.4 %broadcast_select_fusion = bf16[2048,2048]{1,0:T(8,128)(2,1)} fusion(bf16[2048,2048]{1,0:T(8,128)(2,1)} %gather_fusion, pred[2048]{0:T(1024)(128)(4,1)S(1)} %compare_and_fusion), kind=kLoop, calls=%fused_computation.6 | loop fusion | flops 4194304 | bytes 16779264 | tf_op jit(solution)/shard_map/jit(_take)/select_n | solution.py:33
  59.8 12.1 %copy.8 = bf16[2048,2048]{0,1:T(8,128)(2,1)} copy(bf16[2048,2048]{1,0:T(8,128)(2,1)} %broadcast_select_fusion) | data formatting | bytes 16777216 | tf_op jit(solution)/shard_map/jit(_take)/select_n | solution.py:33
  71.9 20.8 %gather_fusion.1 = bf16[2048,2048]{1,0:T(8,128)(2,1)} fusion(bf16[2048,2048]{0,1:T(8,128)(2,1)} %copy.8, s32[2048]{0:T(1024)S(1)} %broadcast_clamp_fusion), kind=kCustom, calls=%fused_computation.3 | custom fusion | bytes 16785408 | tf_op jit(solution)/shard_map/jit(_take)/gather | solution.py:33
  94.9 6.4 %fusion = f32[2048,256]{1,0:T(8,128)S(1)} fusion(bf16[2048,2048]{1,0:T(8,128)(2,1)} %gather_fusion.1, pred[2048]{0:T(1024)(128)(4,1)} %copy-done.9, bf16[512,256]{1,0:T(8,128)(2,1)S(1)} %get-tuple-element.29, bf16[512,256]{1,0:T(8,128)(2,1)S(1)} %neg.13, bf16[512,256]{1,0:T(8,128)(2,1)S(1)} %get-tuple-element.28, bf16[512,256]{1,0:T(8,128)(2,1)S(1)} %neg.12), kind=kOutput, calls=%fused_computation.8 | convolution fusion | flops 2155872256 | bytes 11536384 | tf_op jit(solution)/shard_map/dot_general | solution.py:74
  102.5 2.3 collective-permute-done.8
  105.0 1.7 scatter_fusion
  108.1 6.1 %collective-permute-start.9 = (bf16[512,256]{1,0:T(8,128)(2,1)S(1)}, bf16[512,256]{1,0:T(8,128)(2,1)S(1)}, u32[]{:S(2)}, u32[]{:S(2)}) collective-permute-start(bf16[512,256]{1,0:T(8,128)(2,1)S(1)} %get-tuple-element.24), channel_id=1, source_target_pairs={{1,0},{2,1},{3,2},{5,4},{6,5},{7,6},{9,8},{10,9},{11,10},{13,12},{... | collective-permute-start | bytes 786440 | tf_op jit(solution)/shard_map/ppermute | solution.py:12
  115.0 3.4 %collective-permute-done.9 = bf16[512,256]{1,0:T(8,128)(2,1)S(1)} collective-permute-done((bf16[512,256]{1,0:T(8,128)(2,1)S(1)}, bf16[512,256]{1,0:T(8,128)(2,1)S(1)}, u32[]{:S(2)}, u32[]{:S(2)}) %collective-permute-start.9) | collective-permute-done | bytes 262176 | tf_op jit(solution)/shard_map/ppermute | solution.py:12
  120.5 43.4 %all-reduce = (f32[256]{0:T(256)S(1)}, f32[256]{0:T(256)S(1)}) all-reduce(f32[256]{0:T(256)S(1)} %get-tuple-element.5, f32[256]{0:T(256)S(1)} %get-tuple-element.4), channel_id=1, replica_groups=mesh['sector'=8,'sub'=4] {'sector','sub'}, use_global_device_ids=true, to_apply=%region_1.2 | all-reduce | flops 512 | bytes 4096 | tf_op jit(solution)/shard_map/psum | solution.py:22
  164.1 40.6 %psum.45 = f32[256]{0:T(256)S(1)} all-reduce(f32[256]{0:T(256)S(1)} %multiply_reduce_fusion), channel_id=1, replica_groups=mesh['sector'=8,'sub'=4] {'sector','sub'}, use_global_device_ids=true, to_apply=%region_7.10 | all-reduce | flops 256 | bytes 2048 | tf_op jit(solution)/shard_map/psum | solution.py:22
  205.1 2.6 collective-permute-start.11
  207.7 3.2 %collective-permute-done.12 = bf16[512,256]{1,0:T(8,128)(2,1)S(1)} collective-permute-done((bf16[512,256]{1,0:T(8,128)(2,1)S(1)}, bf16[512,256]{1,0:T(8,128)(2,1)S(1)}, u32[]{:S(2)}, u32[]{:S(2)}) %collective-permute-start.12) | collective-permute-done | bytes 262176 | tf_op jit(solution)/shard_map/ppermute | solution.py:18
  211.0 4.7 %collective-permute-done.11 = bf16[512,256]{1,0:T(8,128)(2,1)S(1)} collective-permute-done((bf16[512,256]{1,0:T(8,128)(2,1)S(1)}, bf16[512,256]{1,0:T(8,128)(2,1)S(1)}, u32[]{:S(2)}, u32[]{:S(2)}) %collective-permute-start.11) | collective-permute-done | bytes 262176 | tf_op jit(solution)/shard_map/ppermute | solution.py:12
  217.3 13.6 %psum.46 = bf16[32,256]{1,0:T(8,128)(2,1)S(1)} all-reduce(bf16[32,256]{1,0:T(8,128)(2,1)S(1)} %broadcast_select_fusion.4), channel_id=1, replica_groups=mesh['sector'=8,'sub'=4] {'sub'}, use_global_device_ids=true, to_apply=%region_8.11 | all-reduce | flops 8192 | bytes 32768 | tf_op jit(solution)/shard_map/psum | solution.py:47
  231.0 3.3 %collective-permute-done.13 = f32[32,256]{1,0:T(8,128)S(1)} collective-permute-done((f32[32,256]{1,0:T(8,128)S(1)}, f32[32,256]{1,0:T(8,128)S(1)}, u32[]{:S(2)}, u32[]{:S(2)}) %collective-permute-start.13) | collective-permute-done | bytes 32800 | tf_op jit(solution)/shard_map/ppermute | solution.py:54
  234.3 1.7 collective-permute-start.17
  236.0 1.6 collective-permute-done.14
  239.4 1.6 collective-permute-done.15
  242.5 7.9 %fusion.1 = f32[2048,256]{1,0:T(8,128)} fusion(bf16[2048,2048]{1,0:T(8,128)(2,1)} %gather_fusion.1, pred[2048]{0:T(1024)(128)(4,1)S(1)} %copy-done.10, bf16[512,256]{1,0:T(8,128)(2,1)} %copy-done.7, bf16[512,256]{1,0:T(8,128)(2,1)} %copy-done.4, bf16[512,256]{1,0:T(8,128)(2,1)} %copy-done.6, bf16[512,256]{1,0:T(8,128)(2,1)} %copy-done.5), kind=kOutput, calls=%fused_computation.9 | convolution fusion | flops 2155872256 | bytes 11536384 | tf_op jit(solution)/shard_map/dot_general | solution.py:74
  250.8 3.6 %collective-permute-done.19 = f32[32,256]{1,0:T(8,128)S(1)} collective-permute-done((f32[32,256]{1,0:T(8,128)S(1)}, f32[32,256]{1,0:T(8,128)S(1)}, u32[]{:S(2)}, u32[]{:S(2)}) %collective-permute-start.19) | collective-permute-done | bytes 32800 | tf_op jit(solution)/shard_map/ppermute | solution.py:56
  254.6 3.7 %scatter_fusion.1 = f32[2048,256]{1,0:T(8,128)} fusion(f32[2048,256]{1,0:T(8,128)} %fusion.1, s32[32]{0:T(128)S(1)} %copy-done.12, f32[32,256]{1,0:T(8,128)S(1)} %convolution_multiply_fusion), kind=kCustom, calls=%fused_computation.5 | custom fusion | flops 8192 | bytes 98432 | tf_op jit(solution)/shard_map/scatter-add | solution.py:73
  258.3 1.8 convert.9
  260.2 6.0 %collective-permute-start.20 = (bf16[512,256]{1,0:T(8,128)(2,1)S(1)}, bf16[512,256]{1,0:T(8,128)(2,1)S(1)}, u32[]{:S(2)}, u32[]{:S(2)}) collective-permute-start(bf16[512,256]{1,0:T(8,128)(2,1)S(1)} %get-tuple-element.22), channel_id=1, source_target_pairs={{1,0},{2,1},{3,2},{5,4},{6,5},{7,6},{9,8},{10,9},{11,10},{13,12},{... | collective-permute-start | bytes 786440 | tf_op jit(solution)/shard_map/ppermute | solution.py:12
  266.3 4.0 %collective-permute-done.20 = bf16[512,256]{1,0:T(8,128)(2,1)S(1)} collective-permute-done((bf16[512,256]{1,0:T(8,128)(2,1)S(1)}, bf16[512,256]{1,0:T(8,128)(2,1)S(1)}, u32[]{:S(2)}, u32[]{:S(2)}) %collective-permute-start.20) | collective-permute-done | bytes 262176 | tf_op jit(solution)/shard_map/ppermute | solution.py:12
  270.9 43.5 %psum.47 = f32[256]{0:T(256)S(1)} all-reduce(f32[256]{0:T(256)S(1)} %fusion.6), channel_id=1, replica_groups=mesh['sector'=8,'sub'=4] {'sector','sub'}, use_global_device_ids=true, to_apply=%region_11.14 | all-reduce | flops 256 | bytes 2048 | tf_op jit(solution)/shard_map/psum | solution.py:86
  314.5 1.6 fusion.7
  (111 shorter events, 18.2 us)
Async XLA Ops:
  0.6 104.1 %copy-start = (f32[256,256]{1,0:T(8,128)S(1)}, f32[256,256]{1,0:T(8,128)}, u32[]{:S(2)}) copy-start(f32[256,256]{1,0:T(8,128)} %param.13) | copy-start | bytes 786436
  2.0 5.8 %collective-permute-start.1 = (bf16[512,256]{1,0:T(8,128)(2,1)S(1)}, bf16[512,256]{1,0:T(8,128)(2,1)S(1)}, u32[]{:S(2)}, u32[]{:S(2)}) collective-permute-start(bf16[512,256]{1,0:T(8,128)(2,1)S(1)} %get-tuple-element.29), channel_id=1, source_target_pairs={{0,4},{4,8},{8,12},{12,16},{16,20},{20,24},{24,28},{28,0},{1,5},{5... | collective-permute-start | bytes 786440 | tf_op jit(solution)/shard_map/ppermute | solution.py:18
  2.1 10.5 %collective-permute-start = (bf16[512,256]{1,0:T(8,128)(2,1)S(1)}, bf16[512,256]{1,0:T(8,128)(2,1)S(1)}, u32[]{:S(2)}, u32[]{:S(2)}) collective-permute-start(bf16[512,256]{1,0:T(8,128)(2,1)S(1)} %get-tuple-element.28), channel_id=1, source_target_pairs={{0,1},{1,2},{2,3},{4,5},{5,6},{6,7},{8,9},{9,10},{10,11},{12,13},{... | collective-permute-start | bytes 786440 | tf_op jit(solution)/shard_map/ppermute | solution.py:12
  5.6 44.0 %copy-start.13 = (pred[32]{0:T(512)(128)(4,1)}, pred[32]{0:T(512)(128)(4,1)S(1)}, u32[]{:S(2)}) copy-start(pred[32]{0:T(512)(128)(4,1)S(1)} %compare_and_fusion.1) | copy-start | bytes 100
  28.8 20.9 %collective-permute-start.2 = (f32[32,256]{1,0:T(8,128)S(1)}, f32[32,256]{1,0:T(8,128)S(1)}, u32[]{:S(2)}, u32[]{:S(2)}) collective-permute-start(f32[32,256]{1,0:T(8,128)S(1)} %convert_element_type.35), channel_id=1, source_target_pairs={{0,4},{4,8},{8,12},{12,16},{16,20},{20,24},{24,28},{28,0},{1,5},{5... | collective-permute-start | bytes 98312 | tf_op jit(solution)/shard_map/ppermute | solution.py:54
  28.8 22.4 %copy-start.9 = (pred[2048]{0:T(1024)(128)(4,1)}, pred[2048]{0:T(1024)(128)(4,1)S(1)}, u32[]{:S(2)}) copy-start(pred[2048]{0:T(1024)(128)(4,1)S(1)} %compare_and_fusion) | copy-start | bytes 6148
  49.7 9.2 %collective-permute-start.3 = (f32[32,256]{1,0:T(8,128)S(1)}, f32[32,256]{1,0:T(8,128)S(1)}, u32[]{:S(2)}, u32[]{:S(2)}) collective-permute-start(f32[32,256]{1,0:T(8,128)S(1)} %collective-permute-done.2), channel_id=1, source_target_pairs={{0,4},{4,8},{8,12},{12,16},{16,20},{20,24},{24,28},{28,0},{1,5},{5... | collective-permute-start | bytes 98312 | tf_op jit(solution)/shard_map/ppermute | solution.py:54
  58.7 34.0 %collective-permute-start.6 = (f32[32,256]{1,0:T(8,128)S(1)}, f32[32,256]{1,0:T(8,128)S(1)}, u32[]{:S(2)}, u32[]{:S(2)}) collective-permute-start(f32[32,256]{1,0:T(8,128)S(1)} %convert_element_type.35), channel_id=1, source_target_pairs={{0,28},{4,0},{8,4},{12,8},{16,12},{20,16},{24,20},{28,24},{1,29},{... | collective-permute-start | bytes 98312 | tf_op jit(solution)/shard_map/ppermute | solution.py:56
  58.9 35.3 %collective-permute-start.4 = (f32[32,256]{1,0:T(8,128)S(1)}, f32[32,256]{1,0:T(8,128)S(1)}, u32[]{:S(2)}, u32[]{:S(2)}) collective-permute-start(f32[32,256]{1,0:T(8,128)S(1)} %collective-permute-done.3), channel_id=1, source_target_pairs={{0,4},{4,8},{8,12},{12,16},{16,20},{20,24},{24,28},{28,0},{1,5},{5... | collective-permute-start | bytes 98312 | tf_op jit(solution)/shard_map/ppermute | solution.py:54
  92.7 8.7 %collective-permute-start.7 = (f32[32,256]{1,0:T(8,128)S(1)}, f32[32,256]{1,0:T(8,128)S(1)}, u32[]{:S(2)}, u32[]{:S(2)}) collective-permute-start(f32[32,256]{1,0:T(8,128)S(1)} %collective-permute-done.6), channel_id=1, source_target_pairs={{0,28},{4,0},{8,4},{12,8},{16,12},{20,16},{24,20},{28,24},{1,29},{... | collective-permute-start | bytes 98312 | tf_op jit(solution)/shard_map/ppermute | solution.py:56
  94.1 8.3 %collective-permute-start.5 = (f32[32,256]{1,0:T(8,128)S(1)}, f32[32,256]{1,0:T(8,128)S(1)}, u32[]{:S(2)}, u32[]{:S(2)}) collective-permute-start(f32[32,256]{1,0:T(8,128)S(1)} %collective-permute-done.4), channel_id=1, source_target_pairs={{0,4},{4,8},{8,12},{12,16},{16,20},{20,24},{24,28},{28,0},{1,5},{5... | collective-permute-start | bytes 98312 | tf_op jit(solution)/shard_map/ppermute | solution.py:54
  101.4 3.3 %collective-permute-start.8 = (f32[32,256]{1,0:T(8,128)S(1)}, f32[32,256]{1,0:T(8,128)S(1)}, u32[]{:S(2)}, u32[]{:S(2)}) collective-permute-start(f32[32,256]{1,0:T(8,128)S(1)} %collective-permute-done.7), channel_id=1, source_target_pairs={{0,28},{4,0},{8,4},{12,8},{16,12},{20,16},{24,20},{28,24},{1,29},{... | collective-permute-start | bytes 98312 | tf_op jit(solution)/shard_map/ppermute | solution.py:56
  108.1 12.1 %copy-start.1 = (f32[1,1,2,512,256]{4,3,2,1,0:T(8,128)S(1)}, f32[1,1,2,512,256]{4,3,2,1,0:T(8,128)}, u32[]{:S(2)}) copy-start(f32[1,1,2,512,256]{4,3,2,1,0:T(8,128)} %param.9) | copy-start | bytes 3145732
  108.1 10.2 %collective-permute-start.9 = (bf16[512,256]{1,0:T(8,128)(2,1)S(1)}, bf16[512,256]{1,0:T(8,128)(2,1)S(1)}, u32[]{:S(2)}, u32[]{:S(2)}) collective-permute-start(bf16[512,256]{1,0:T(8,128)(2,1)S(1)} %get-tuple-element.24), channel_id=1, source_target_pairs={{1,0},{2,1},{3,2},{5,4},{6,5},{7,6},{9,8},{10,9},{11,10},{13,12},{... | collective-permute-start | bytes 786440 | tf_op jit(solution)/shard_map/ppermute | solution.py:12
  114.3 4.6 %collective-permute-start.10 = (bf16[512,256]{1,0:T(8,128)(2,1)S(1)}, bf16[512,256]{1,0:T(8,128)(2,1)S(1)}, u32[]{:S(2)}, u32[]{:S(2)}) collective-permute-start(bf16[512,256]{1,0:T(8,128)(2,1)S(1)} %get-tuple-element.25), channel_id=1, source_target_pairs={{0,28},{4,0},{8,4},{12,8},{16,12},{20,16},{24,20},{28,24},{1,29},{... | collective-permute-start | bytes 786440 | tf_op jit(solution)/shard_map/ppermute | solution.py:18
  205.0 12.3 %copy-start.14 = (pred[32]{0:T(512)(128)(4,1)S(1)}, pred[32]{0:T(512)(128)(4,1)}, u32[]{:S(2)}) copy-start(pred[32]{0:T(512)(128)(4,1)} %copy-done.13) | copy-start | bytes 100
  205.0 37.5 %copy-start.10 = (pred[2048]{0:T(1024)(128)(4,1)S(1)}, pred[2048]{0:T(1024)(128)(4,1)}, u32[]{:S(2)}) copy-start(pred[2048]{0:T(1024)(128)(4,1)} %copy-done.9) | copy-start | bytes 6148
  205.0 10.6 %copy-start.6 = (bf16[512,256]{1,0:T(8,128)(2,1)}, bf16[512,256]{1,0:T(8,128)(2,1)S(1)}, u32[]{:S(2)}) copy-start(bf16[512,256]{1,0:T(8,128)(2,1)S(1)} %get-tuple-element.26) | copy-start | bytes 786436
  205.0 10.6 %copy-start.7 = (bf16[512,256]{1,0:T(8,128)(2,1)}, bf16[512,256]{1,0:T(8,128)(2,1)S(1)}, u32[]{:S(2)}) copy-start(bf16[512,256]{1,0:T(8,128)(2,1)S(1)} %get-tuple-element.27) | copy-start | bytes 786436
  205.1 5.8 %collective-permute-start.12 = (bf16[512,256]{1,0:T(8,128)(2,1)S(1)}, bf16[512,256]{1,0:T(8,128)(2,1)S(1)}, u32[]{:S(2)}, u32[]{:S(2)}) collective-permute-start(bf16[512,256]{1,0:T(8,128)(2,1)S(1)} %get-tuple-element.27), channel_id=1, source_target_pairs={{0,4},{4,8},{8,12},{12,16},{16,20},{20,24},{24,28},{28,0},{1,5},{5... | collective-permute-start | bytes 786440 | tf_op jit(solution)/shard_map/ppermute | solution.py:18
  205.1 10.5 %collective-permute-start.11 = (bf16[512,256]{1,0:T(8,128)(2,1)S(1)}, bf16[512,256]{1,0:T(8,128)(2,1)S(1)}, u32[]{:S(2)}, u32[]{:S(2)}) collective-permute-start(bf16[512,256]{1,0:T(8,128)(2,1)S(1)} %get-tuple-element.26), channel_id=1, source_target_pairs={{0,1},{1,2},{2,3},{4,5},{5,6},{6,7},{8,9},{9,10},{10,11},{12,13},{... | collective-permute-start | bytes 786440 | tf_op jit(solution)/shard_map/ppermute | solution.py:12
  230.9 23.7 %copy-start.12 = (s32[32]{0:T(128)S(1)}, s32[32]{0:T(128)}, u32[]{:S(2)}) copy-start(s32[32]{0:T(128)} %fusion.25) | copy-start | bytes 388
  230.9 3.4 %collective-permute-start.13 = (f32[32,256]{1,0:T(8,128)S(1)}, f32[32,256]{1,0:T(8,128)S(1)}, u32[]{:S(2)}, u32[]{:S(2)}) collective-permute-start(f32[32,256]{1,0:T(8,128)S(1)} %convert_element_type.39), channel_id=1, source_target_pairs={{0,4},{4,8},{8,12},{12,16},{16,20},{20,24},{24,28},{28,0},{1,5},{5... | collective-permute-start | bytes 98312 | tf_op jit(solution)/shard_map/ppermute | solution.py:54
  234.3 3.3 %collective-permute-start.14 = (f32[32,256]{1,0:T(8,128)S(1)}, f32[32,256]{1,0:T(8,128)S(1)}, u32[]{:S(2)}, u32[]{:S(2)}) collective-permute-start(f32[32,256]{1,0:T(8,128)S(1)} %collective-permute-done.13), channel_id=1, source_target_pairs={{0,4},{4,8},{8,12},{12,16},{16,20},{20,24},{24,28},{28,0},{1,5},{5... | collective-permute-start | bytes 98312 | tf_op jit(solution)/shard_map/ppermute | solution.py:54
  234.3 3.9 %collective-permute-start.17 = (f32[32,256]{1,0:T(8,128)S(1)}, f32[32,256]{1,0:T(8,128)S(1)}, u32[]{:S(2)}, u32[]{:S(2)}) collective-permute-start(f32[32,256]{1,0:T(8,128)S(1)} %convert_element_type.39), channel_id=1, source_target_pairs={{0,28},{4,0},{8,4},{12,8},{16,12},{20,16},{24,20},{28,24},{1,29},{... | collective-permute-start | bytes 98312 | tf_op jit(solution)/shard_map/ppermute | solution.py:56
  237.6 3.3 %collective-permute-start.15 = (f32[32,256]{1,0:T(8,128)S(1)}, f32[32,256]{1,0:T(8,128)S(1)}, u32[]{:S(2)}, u32[]{:S(2)}) collective-permute-start(f32[32,256]{1,0:T(8,128)S(1)} %collective-permute-done.14), channel_id=1, source_target_pairs={{0,4},{4,8},{8,12},{12,16},{16,20},{20,24},{24,28},{28,0},{1,5},{5... | collective-permute-start | bytes 98312 | tf_op jit(solution)/shard_map/ppermute | solution.py:54
  238.2 12.2 %collective-permute-start.18 = (f32[32,256]{1,0:T(8,128)S(1)}, f32[32,256]{1,0:T(8,128)S(1)}, u32[]{:S(2)}, u32[]{:S(2)}) collective-permute-start(f32[32,256]{1,0:T(8,128)S(1)} %collective-permute-done.17), channel_id=1, source_target_pairs={{0,28},{4,0},{8,4},{12,8},{16,12},{20,16},{24,20},{28,24},{1,29},{... | collective-permute-start | bytes 98312 | tf_op jit(solution)/shard_map/ppermute | solution.py:56
  241.0 9.7 %collective-permute-start.16 = (f32[32,256]{1,0:T(8,128)S(1)}, f32[32,256]{1,0:T(8,128)S(1)}, u32[]{:S(2)}, u32[]{:S(2)}) collective-permute-start(f32[32,256]{1,0:T(8,128)S(1)} %collective-permute-done.15), channel_id=1, source_target_pairs={{0,4},{4,8},{8,12},{12,16},{16,20},{20,24},{24,28},{28,0},{1,5},{5... | collective-permute-start | bytes 98312 | tf_op jit(solution)/shard_map/ppermute | solution.py:54
  250.4 3.9 %collective-permute-start.19 = (f32[32,256]{1,0:T(8,128)S(1)}, f32[32,256]{1,0:T(8,128)S(1)}, u32[]{:S(2)}, u32[]{:S(2)}) collective-permute-start(f32[32,256]{1,0:T(8,128)S(1)} %collective-permute-done.18), channel_id=1, source_target_pairs={{0,28},{4,0},{8,4},{12,8},{16,12},{20,16},{24,20},{28,24},{1,29},{... | collective-permute-start | bytes 98312 | tf_op jit(solution)/shard_map/ppermute | solution.py:56
  258.3 12.2 %copy-start.2 = (f32[2048,256]{1,0:T(8,128)S(1)}, f32[2048,256]{1,0:T(8,128)}, u32[]{:S(2)}) copy-start(f32[2048,256]{1,0:T(8,128)} %scatter_fusion.1) | copy-start | bytes 6291460
  260.2 10.1 %collective-permute-start.20 = (bf16[512,256]{1,0:T(8,128)(2,1)S(1)}, bf16[512,256]{1,0:T(8,128)(2,1)S(1)}, u32[]{:S(2)}, u32[]{:S(2)}) collective-permute-start(bf16[512,256]{1,0:T(8,128)(2,1)S(1)} %get-tuple-element.22), channel_id=1, source_target_pairs={{1,0},{2,1},{3,2},{5,4},{6,5},{7,6},{9,8},{10,9},{11,10},{13,12},{... | collective-permute-start | bytes 786440 | tf_op jit(solution)/shard_map/ppermute | solution.py:12
  266.2 4.3 %collective-permute-start.21 = (bf16[512,256]{1,0:T(8,128)(2,1)S(1)}, bf16[512,256]{1,0:T(8,128)(2,1)S(1)}, u32[]{:S(2)}, u32[]{:S(2)}) collective-permute-start(bf16[512,256]{1,0:T(8,128)(2,1)S(1)} %get-tuple-element.23), channel_id=1, source_target_pairs={{0,28},{4,0},{8,4},{12,8},{16,12},{20,16},{24,20},{28,24},{1,29},{... | collective-permute-start | bytes 786440 | tf_op jit(solution)/shard_map/ppermute | solution.py:18
  (6 other events, 23.8 us)
